TPU v7x, 512 devices: a whole 4x8x8 slice. The times are simulated.
512 devices in a mesh: section: 16 (over x_hi, y), dp: 8 (over z), mp: 4 (over x_lo, core).
Axes of the slice: x: 4 (x_hi: 2, x_lo: 2; x = x_hi * 2 + x_lo), y: 8, z: 8, core: 2. Of those that a mesh axis runs over, the one named last changes fastest.
Arguments:
- cotangent: bfloat16 [1024, 4096], P('dp', 'mp'), may hold values from -6 to 6
- saved_inputs: bfloat16 [16, 1024, 4096], P('section', 'dp', 'mp'), may hold values from -6 to 6
- pre_acts: bfloat16 [16, 1024, 4096], P('section', 'dp', 'mp'), may hold values from -8 to 8
- weights: bfloat16 [16, 4096, 4096], P('section', 'mp', 'dp'), may hold values from -0.046875 to 0.046875
- proj_in: bfloat16 [16, 4096, 64], P('section', 'mp'), may hold values from -0.09375 to 0.09375
- proj_out: bfloat16 [16, 4096, 64], P('section', 'mp'), may hold values from -0.09375 to 0.09375
- query_panels: float32 [16, 16, 4096], P('section', 'dp', 'mp'), may hold values from -4 to 4
- partners: int32 [8, 8], replicated, may hold values from 0 to 7, as said below
Outputs:
- train_panels: float32 [16, 32, 4096], P('section', 'dp', 'mp')
- scores: float32 [16, 8, 4], replicated
Inputs may be any that keep to these rules, and one draw needn't show every extreme that they name: The plan has 8 rounds: one round pairs every dp index with itself, and the others are the rounds of one round-robin plan of the 8 indices. The rows of partners hold each of these rounds once, in some order, so partners[r, partners[r, i]] = i.
All inputs are finite; a program needn't handle non-finite values.
Results may differ from a plain program's by a relative error of at most 0.02.
Values may be sent and summed in bfloat16 or wider, within the bound.
No kernel may reach another device: no remote copies, remote signals or barrier semaphores. Data moves between devices by JAX's collectives and lax.ppermute only.
A program may use at most 64 MiB of HBM per device.

v0:
```python
import math
import jax
import jax.numpy as jnp
from jax import lax
from jax.sharding import PartitionSpec as P

LEN = 32


def from_behind(block, axis, distance):
    devices = range(lax.axis_size(axis))
    route = [(i - distance, i) for i in devices if i - distance in devices]
    return lax.ppermute(block, axis, route)


def silu_slope(pre_state):
    sigma = jax.nn.sigmoid(pre_state)
    return sigma * (1.0 + pre_state * (1.0 - sigma))


def score_pair(query_rows, train_rows):
    return jnp.dot(query_rows, train_rows.T, precision=lax.Precision.HIGHEST)


def place_block(score_table, block, row_at, col_at):
    return lax.dynamic_update_slice(
        score_table,
        block[None, None],
        (jnp.asarray(row_at, jnp.int32), jnp.int32(col_at), jnp.int32(0), jnp.int32(0)),
    )


def body(cotangent, saved_inputs, pre_acts, weights, proj_in, proj_out, query_panels, partners):
    section_count = lax.axis_size("section")
    model_count = lax.axis_size("mp")
    data_count = lax.axis_size("dp")
    section_index = lax.axis_index("section")
    model_index = lax.axis_index("mp")
    data_index = lax.axis_index("dp")
    inputs = saved_inputs[0]
    pre_state = pre_acts[0]
    columns = inputs.shape[1]
    length = LEN
    examples = inputs.shape[0] // length
    low_rank = proj_in.shape[2]
    w_rows = lax.all_gather(weights[0], "dp", axis=1, tiled=True)
    step_count = examples + section_count - 1
    top_section = section_count - 1

    def advance(turn, carry):
        outgoing, stored, side_store = carry
        received = from_behind(outgoing, "section", -1)
        example_at = turn - (top_section - section_index)
        active = jnp.logical_and(example_at >= 0, example_at < examples)
        row_start = jnp.clip(example_at, 0, examples - 1) * length
        top_grad = lax.dynamic_slice_in_dim(cotangent, row_start, length, 0)
        delta_piece = jnp.where(section_index == top_section, top_grad, received)
        slopes = silu_slope(
            lax.dynamic_slice_in_dim(pre_state, row_start, length, 0).astype(jnp.float32)
        )
        grad_piece = (delta_piece.astype(jnp.float32) * slopes).astype(jnp.bfloat16)
        grad_full = lax.all_gather(grad_piece, "mp", axis=1, tiled=True)

        def through():
            back_term = lax.dot_general(
                grad_full, w_rows, (((1,), (1,)), ((), ())), preferred_element_type=jnp.float32
            )
            return (delta_piece.astype(jnp.float32) + back_term).astype(jnp.bfloat16)

        def skipped():
            return jnp.zeros_like(delta_piece)

        passed = lax.cond(active, through, skipped)
        previous = lax.dynamic_slice_in_dim(stored, row_start, length, 0)
        stored = lax.dynamic_update_slice_in_dim(
            stored, jnp.where(active, grad_piece, previous), row_start, 0
        )
        return (passed, stored, side_store)

    initial = (
        jnp.zeros((length, columns), jnp.bfloat16),
        jnp.zeros((inputs.shape[0], columns), jnp.bfloat16),
        jnp.zeros((inputs.shape[0], low_rank), jnp.float32),
    )
    final_state = lax.fori_loop(0, step_count, advance, initial)
    stored = final_state[1]
    side_store = final_state[2]
    in_part = jnp.dot(inputs, proj_in[0], preferred_element_type=jnp.float32)
    out_part = jnp.dot(stored, proj_out[0], preferred_element_type=jnp.float32)
    in_side, out_side = (
        lax.psum(in_part.astype(jnp.bfloat16), "mp").astype(jnp.float32),
        lax.psum(out_part.astype(jnp.bfloat16), "mp").astype(jnp.float32),
    )
    piece_rank = low_rank // model_count
    in_rows = lax.dynamic_slice_in_dim(in_side, model_index * piece_rank, piece_rank, 1)
    panels_here = jnp.einsum(
        "etr,etc->erc",
        in_rows.reshape(examples, length, piece_rank),
        out_side.reshape(examples, length, low_rank),
        precision=lax.Precision.HIGHEST,
    ) / math.sqrt(length)
    panels_here = panels_here.reshape(examples, piece_rank * low_rank)
    queries = query_panels[0]
    asked = queries.shape[0]
    rounds = partners.shape[0]
    score_scale = 1.0 / (low_rank * math.sqrt(section_count))
    score_table = jnp.zeros((data_count, rounds, asked, examples), jnp.float32)
    everyone = lax.all_gather(panels_here, "dp", axis=0, tiled=True).reshape(
        data_count, examples, -1
    )
    for round_at in range(rounds):
        partner = partners[round_at, data_index]
        chosen = lax.dynamic_index_in_dim(everyone, partner, 0, keepdims=False)
        score_table = place_block(score_table, score_pair(queries, chosen), data_index, round_at)
    summed = lax.psum(score_table * score_scale, ("section", "dp", "mp"))
    scores = summed.transpose(0, 2, 1, 3).reshape(data_count * asked, rounds, examples)
    return (panels_here[None], scores)


def solution(mesh):
    placed = (
        P("dp", "mp"),
        P("section", "dp", "mp"),
        P("section", "dp", "mp"),
        P("section", "mp", "dp"),
        P("section", "mp", None),
        P("section", "mp", None),
        P("section", "dp", "mp"),
        P(),
    )
    return jax.shard_map(
        body, mesh=mesh, in_specs=placed, out_specs=(P("section", "dp", "mp"), P()), check_vma=False
    )
```

profile of v0, /device:TPU:1, one launch (start us, length us, event | category | flops | bytes accessed | tf_op | source)
XLA Modules:
  0.0 635.7 jit_solution(11931362347134518088)
XLA Ops:
  7.9 1.7 constant_dynamic-slice_fusion.2
  25.3 87.9 %all-gather.4.cloned.1.call-done = bf16[1,1024,4096]{2,1,0:T(8,128)(2,1)} async-done(((bf16[1,1024,512]{2,1,0:T(8,128)(2,1)}), bf16[1,1024,4096]{2,1,0:T(8,128)(2,1)}) %all-gather.4.cloned.1.call-update) | async-done | bytes 8388624 | tf_op jit(solution)/shard_map/all_gather | solution.py:46
  113.8 380.4 %while.17 = (s32[]{:T(128)}, bf16[32,1024]{1,0:T(8,128)(2,1)}, bf16[128,1024]{1,0:T(8,128)(2,1)S(1)}, s32[]{:T(128)}, pred[]{:T(512)}, /*index=5*/bf16[128,1024]...) while((s32[]{:T(128)}, bf16[32,1024]{1,0:T(8,128)(2,1)}, ...), condition=%wide.region_4.5_spmd, body=%wide.region_1.4_spmd.sunk | while | flops 268959744 | bytes 9830719 | solution.py:85
  113.9 1.4 collective-permute-start
  115.3 3.9 collective-permute-done
  120.2 7.4 %all_gather.18 = bf16[32,4096]{1,0:T(8,128)(2,1)S(1)} all-gather(bf16[32,1024]{1,0:T(8,128)(2,1)S(1)} %get-tuple-element.282), channel_id=1, replica_groups=mesh['section'=16,'dp'=8,'mp'=4] {'mp'}, dimensions={1}, use_global_device_ids=true | all-gather | bytes 327680 | tf_op jit(solution)/shard_map/while/body/eval_jaxpr/all_gather | solution.py:62
  128.2 1.3 collective-permute-start
  129.6 4.3 collective-permute-done
  134.8 6.6 %all_gather.18 = bf16[32,4096]{1,0:T(8,128)(2,1)S(1)} all-gather(bf16[32,1024]{1,0:T(8,128)(2,1)S(1)} %get-tuple-element.282), channel_id=1, replica_groups=mesh['section'=16,'dp'=8,'mp'=4] {'mp'}, dimensions={1}, use_global_device_ids=true | all-gather | bytes 327680 | tf_op jit(solution)/shard_map/while/body/eval_jaxpr/all_gather | solution.py:62
  142.1 1.3 collective-permute-start
  143.4 4.3 collective-permute-done
  148.7 6.6 %all_gather.18 = bf16[32,4096]{1,0:T(8,128)(2,1)S(1)} all-gather(bf16[32,1024]{1,0:T(8,128)(2,1)S(1)} %get-tuple-element.282), channel_id=1, replica_groups=mesh['section'=16,'dp'=8,'mp'=4] {'mp'}, dimensions={1}, use_global_device_ids=true | all-gather | bytes 327680 | tf_op jit(solution)/shard_map/while/body/eval_jaxpr/all_gather | solution.py:62
  155.9 1.3 collective-permute-start
  157.2 5.0 collective-permute-done
  163.2 6.4 %all_gather.18 = bf16[32,4096]{1,0:T(8,128)(2,1)S(1)} all-gather(bf16[32,1024]{1,0:T(8,128)(2,1)S(1)} %get-tuple-element.282), channel_id=1, replica_groups=mesh['section'=16,'dp'=8,'mp'=4] {'mp'}, dimensions={1}, use_global_device_ids=true | all-gather | bytes 327680 | tf_op jit(solution)/shard_map/while/body/eval_jaxpr/all_gather | solution.py:62
  170.1 1.3 collective-permute-start
  171.5 5.8 collective-permute-done
  178.2 6.4 %all_gather.18 = bf16[32,4096]{1,0:T(8,128)(2,1)S(1)} all-gather(bf16[32,1024]{1,0:T(8,128)(2,1)S(1)} %get-tuple-element.282), channel_id=1, replica_groups=mesh['section'=16,'dp'=8,'mp'=4] {'mp'}, dimensions={1}, use_global_device_ids=true | all-gather | bytes 327680 | tf_op jit(solution)/shard_map/while/body/eval_jaxpr/all_gather | solution.py:62
  185.2 1.3 collective-permute-start
  186.5 5.8 collective-permute-done
  193.2 6.4 %all_gather.18 = bf16[32,4096]{1,0:T(8,128)(2,1)S(1)} all-gather(bf16[32,1024]{1,0:T(8,128)(2,1)S(1)} %get-tuple-element.282), channel_id=1, replica_groups=mesh['section'=16,'dp'=8,'mp'=4] {'mp'}, dimensions={1}, use_global_device_ids=true | all-gather | bytes 327680 | tf_op jit(solution)/shard_map/while/body/eval_jaxpr/all_gather | solution.py:62
  200.2 1.3 collective-permute-start
  201.5 5.8 collective-permute-done
  208.2 6.4 %all_gather.18 = bf16[32,4096]{1,0:T(8,128)(2,1)S(1)} all-gather(bf16[32,1024]{1,0:T(8,128)(2,1)S(1)} %get-tuple-element.282), channel_id=1, replica_groups=mesh['section'=16,'dp'=8,'mp'=4] {'mp'}, dimensions={1}, use_global_device_ids=true | all-gather | bytes 327680 | tf_op jit(solution)/shard_map/while/body/eval_jaxpr/all_gather | solution.py:62
  215.2 1.3 collective-permute-start
  216.5 5.8 collective-permute-done
  223.2 6.4 %all_gather.18 = bf16[32,4096]{1,0:T(8,128)(2,1)S(1)} all-gather(bf16[32,1024]{1,0:T(8,128)(2,1)S(1)} %get-tuple-element.282), channel_id=1, replica_groups=mesh['section'=16,'dp'=8,'mp'=4] {'mp'}, dimensions={1}, use_global_device_ids=true | all-gather | bytes 327680 | tf_op jit(solution)/shard_map/while/body/eval_jaxpr/all_gather | solution.py:62
  230.2 1.3 collective-permute-start
  231.5 5.8 collective-permute-done
  238.3 6.4 %all_gather.18 = bf16[32,4096]{1,0:T(8,128)(2,1)S(1)} all-gather(bf16[32,1024]{1,0:T(8,128)(2,1)S(1)} %get-tuple-element.282), channel_id=1, replica_groups=mesh['section'=16,'dp'=8,'mp'=4] {'mp'}, dimensions={1}, use_global_device_ids=true | all-gather | bytes 327680 | tf_op jit(solution)/shard_map/while/body/eval_jaxpr/all_gather | solution.py:62
  245.3 1.3 collective-permute-start
  246.6 5.8 collective-permute-done
  253.3 6.4 %all_gather.18 = bf16[32,4096]{1,0:T(8,128)(2,1)S(1)} all-gather(bf16[32,1024]{1,0:T(8,128)(2,1)S(1)} %get-tuple-element.282), channel_id=1, replica_groups=mesh['section'=16,'dp'=8,'mp'=4] {'mp'}, dimensions={1}, use_global_device_ids=true | all-gather | bytes 327680 | tf_op jit(solution)/shard_map/while/body/eval_jaxpr/all_gather | solution.py:62
  260.3 1.3 collective-permute-start
  261.6 8.1 %collective-permute-done = bf16[32,1024]{1,0:T(8,128)(2,1)S(1)} collective-permute-done((bf16[32,1024]{1,0:T(8,128)(2,1)}, bf16[32,1024]{1,0:T(8,128)(2,1)S(1)}, u32[]{:S(2)}, u32[]{:S(2)}) %collective-permute-start) | collective-permute-done | bytes 65568 | tf_op jit(solution)/shard_map/while/body/eval_jaxpr/ppermute | solution.py:13
  270.6 6.4 %all_gather.18 = bf16[32,4096]{1,0:T(8,128)(2,1)S(1)} all-gather(bf16[32,1024]{1,0:T(8,128)(2,1)S(1)} %get-tuple-element.282), channel_id=1, replica_groups=mesh['section'=16,'dp'=8,'mp'=4] {'mp'}, dimensions={1}, use_global_device_ids=true | all-gather | bytes 327680 | tf_op jit(solution)/shard_map/while/body/eval_jaxpr/all_gather | solution.py:62
  277.6 1.3 collective-permute-start
  278.9 8.2 %collective-permute-done = bf16[32,1024]{1,0:T(8,128)(2,1)S(1)} collective-permute-done((bf16[32,1024]{1,0:T(8,128)(2,1)}, bf16[32,1024]{1,0:T(8,128)(2,1)S(1)}, u32[]{:S(2)}, u32[]{:S(2)}) %collective-permute-start) | collective-permute-done | bytes 65568 | tf_op jit(solution)/shard_map/while/body/eval_jaxpr/ppermute | solution.py:13
  288.0 6.4 %all_gather.18 = bf16[32,4096]{1,0:T(8,128)(2,1)S(1)} all-gather(bf16[32,1024]{1,0:T(8,128)(2,1)S(1)} %get-tuple-element.282), channel_id=1, replica_groups=mesh['section'=16,'dp'=8,'mp'=4] {'mp'}, dimensions={1}, use_global_device_ids=true | all-gather | bytes 327680 | tf_op jit(solution)/shard_map/while/body/eval_jaxpr/all_gather | solution.py:62
  296.3 8.2 %collective-permute-done = bf16[32,1024]{1,0:T(8,128)(2,1)S(1)} collective-permute-done((bf16[32,1024]{1,0:T(8,128)(2,1)}, bf16[32,1024]{1,0:T(8,128)(2,1)S(1)}, u32[]{:S(2)}, u32[]{:S(2)}) %collective-permute-start) | collective-permute-done | bytes 65568 | tf_op jit(solution)/shard_map/while/body/eval_jaxpr/ppermute | solution.py:13
  305.5 6.4 %all_gather.18 = bf16[32,4096]{1,0:T(8,128)(2,1)S(1)} all-gather(bf16[32,1024]{1,0:T(8,128)(2,1)S(1)} %get-tuple-element.282), channel_id=1, replica_groups=mesh['section'=16,'dp'=8,'mp'=4] {'mp'}, dimensions={1}, use_global_device_ids=true | all-gather | bytes 327680 | tf_op jit(solution)/shard_map/while/body/eval_jaxpr/all_gather | solution.py:62
  313.8 8.2 %collective-permute-done = bf16[32,1024]{1,0:T(8,128)(2,1)S(1)} collective-permute-done((bf16[32,1024]{1,0:T(8,128)(2,1)}, bf16[32,1024]{1,0:T(8,128)(2,1)S(1)}, u32[]{:S(2)}, u32[]{:S(2)}) %collective-permute-start) | collective-permute-done | bytes 65568 | tf_op jit(solution)/shard_map/while/body/eval_jaxpr/ppermute | solution.py:13
  322.9 6.4 %all_gather.18 = bf16[32,4096]{1,0:T(8,128)(2,1)S(1)} all-gather(bf16[32,1024]{1,0:T(8,128)(2,1)S(1)} %get-tuple-element.282), channel_id=1, replica_groups=mesh['section'=16,'dp'=8,'mp'=4] {'mp'}, dimensions={1}, use_global_device_ids=true | all-gather | bytes 327680 | tf_op jit(solution)/shard_map/while/body/eval_jaxpr/all_gather | solution.py:62
  331.2 8.2 %collective-permute-done = bf16[32,1024]{1,0:T(8,128)(2,1)S(1)} collective-permute-done((bf16[32,1024]{1,0:T(8,128)(2,1)}, bf16[32,1024]{1,0:T(8,128)(2,1)S(1)}, u32[]{:S(2)}, u32[]{:S(2)}) %collective-permute-start) | collective-permute-done | bytes 65568 | tf_op jit(solution)/shard_map/while/body/eval_jaxpr/ppermute | solution.py:13
  340.3 6.4 %all_gather.18 = bf16[32,4096]{1,0:T(8,128)(2,1)S(1)} all-gather(bf16[32,1024]{1,0:T(8,128)(2,1)S(1)} %get-tuple-element.282), channel_id=1, replica_groups=mesh['section'=16,'dp'=8,'mp'=4] {'mp'}, dimensions={1}, use_global_device_ids=true | all-gather | bytes 327680 | tf_op jit(solution)/shard_map/while/body/eval_jaxpr/all_gather | solution.py:62
  348.6 61.6 %collective-permute-done = bf16[32,1024]{1,0:T(8,128)(2,1)S(1)} collective-permute-done((bf16[32,1024]{1,0:T(8,128)(2,1)}, bf16[32,1024]{1,0:T(8,128)(2,1)S(1)}, u32[]{:S(2)}, u32[]{:S(2)}) %collective-permute-start) | collective-permute-done | bytes 65568 | tf_op jit(solution)/shard_map/while/body/eval_jaxpr/ppermute | solution.py:13
  411.2 6.3 all_gather.18
  417.5 6.6 %conditional.2 = (bf16[32,1024]{1,0:T(8,128)(2,1)}) conditional(s32[]{:T(128)} %convert_element_type.80, () %tuple.60, (bf16[32,1024]{1,0:T(8,128)(2,1)S(1)}, bf16[32,4096]{1,0:T(8,128)(2,1)S(1)}, bf16[1024,4096]{1,0:T(8,128)(2,1)}) %tuple.61), branch_computations={%region_2.2_spmd, %region_3.3_spmd} | conditional | flops 268533760 | bytes 8781832 | solution.py:73
  417.5 6.6 %fusion = bf16[32,1024]{1,0:T(8,128)(2,1)} fusion(bf16[32,4096]{1,0:T(8,128)(2,1)S(1)} %get-tuple-element.181, bf16[1024,4096]{1,0:T(8,128)(2,1)} %get-tuple-element.182, bf16[32,1024]{1,0:T(8,128)(2,1)S(1)} %get-tuple-element.180), kind=kOutput, calls=%fused_computation.1 | convolution fusion | flops 268533760 | bytes 8781824 | tf_op jit(solution)/shard_map/while/body/eval_jaxpr/cond/branch_1_fun/dot_general | solution.py:65
  425.4 8.2 %collective-permute-done = bf16[32,1024]{1,0:T(8,128)(2,1)S(1)} collective-permute-done((bf16[32,1024]{1,0:T(8,128)(2,1)}, bf16[32,1024]{1,0:T(8,128)(2,1)S(1)}, u32[]{:S(2)}, u32[]{:S(2)}) %collective-permute-start) | collective-permute-done | bytes 65568 | tf_op jit(solution)/shard_map/while/body/eval_jaxpr/ppermute | solution.py:13
  434.6 6.3 all_gather.18
  440.8 6.6 %conditional.2 = (bf16[32,1024]{1,0:T(8,128)(2,1)}) conditional(s32[]{:T(128)} %convert_element_type.80, () %tuple.60, (bf16[32,1024]{1,0:T(8,128)(2,1)S(1)}, bf16[32,4096]{1,0:T(8,128)(2,1)S(1)}, bf16[1024,4096]{1,0:T(8,128)(2,1)}) %tuple.61), branch_computations={%region_2.2_spmd, %region_3.3_spmd} | conditional | flops 268533760 | bytes 8781832 | solution.py:73
  440.8 6.6 %fusion = bf16[32,1024]{1,0:T(8,128)(2,1)} fusion(bf16[32,4096]{1,0:T(8,128)(2,1)S(1)} %get-tuple-element.181, bf16[1024,4096]{1,0:T(8,128)(2,1)} %get-tuple-element.182, bf16[32,1024]{1,0:T(8,128)(2,1)S(1)} %get-tuple-element.180), kind=kOutput, calls=%fused_computation.1 | convolution fusion | flops 268533760 | bytes 8781824 | tf_op jit(solution)/shard_map/while/body/eval_jaxpr/cond/branch_1_fun/dot_general | solution.py:65
  448.7 8.3 %collective-permute-done = bf16[32,1024]{1,0:T(8,128)(2,1)S(1)} collective-permute-done((bf16[32,1024]{1,0:T(8,128)(2,1)}, bf16[32,1024]{1,0:T(8,128)(2,1)S(1)}, u32[]{:S(2)}, u32[]{:S(2)}) %collective-permute-start) | collective-permute-done | bytes 65568 | tf_op jit(solution)/shard_map/while/body/eval_jaxpr/ppermute | solution.py:13
  458.0 6.3 all_gather.18
  464.3 6.6 %conditional.2 = (bf16[32,1024]{1,0:T(8,128)(2,1)}) conditional(s32[]{:T(128)} %convert_element_type.80, () %tuple.60, (bf16[32,1024]{1,0:T(8,128)(2,1)S(1)}, bf16[32,4096]{1,0:T(8,128)(2,1)S(1)}, bf16[1024,4096]{1,0:T(8,128)(2,1)}) %tuple.61), branch_computations={%region_2.2_spmd, %region_3.3_spmd} | conditional | flops 268533760 | bytes 8781832 | solution.py:73
  464.3 6.6 %fusion = bf16[32,1024]{1,0:T(8,128)(2,1)} fusion(bf16[32,4096]{1,0:T(8,128)(2,1)S(1)} %get-tuple-element.181, bf16[1024,4096]{1,0:T(8,128)(2,1)} %get-tuple-element.182, bf16[32,1024]{1,0:T(8,128)(2,1)S(1)} %get-tuple-element.180), kind=kOutput, calls=%fused_computation.1 | convolution fusion | flops 268533760 | bytes 8781824 | tf_op jit(solution)/shard_map/while/body/eval_jaxpr/cond/branch_1_fun/dot_general | solution.py:65
  472.2 8.2 %collective-permute-done = bf16[32,1024]{1,0:T(8,128)(2,1)S(1)} collective-permute-done((bf16[32,1024]{1,0:T(8,128)(2,1)}, bf16[32,1024]{1,0:T(8,128)(2,1)S(1)}, u32[]{:S(2)}, u32[]{:S(2)}) %collective-permute-start) | collective-permute-done | bytes 65568 | tf_op jit(solution)/shard_map/while/body/eval_jaxpr/ppermute | solution.py:13
  481.4 6.3 all_gather.18
  487.7 6.6 %conditional.2 = (bf16[32,1024]{1,0:T(8,128)(2,1)}) conditional(s32[]{:T(128)} %convert_element_type.80, () %tuple.60, (bf16[32,1024]{1,0:T(8,128)(2,1)S(1)}, bf16[32,4096]{1,0:T(8,128)(2,1)S(1)}, bf16[1024,4096]{1,0:T(8,128)(2,1)}) %tuple.61), branch_computations={%region_2.2_spmd, %region_3.3_spmd} | conditional | flops 268533760 | bytes 8781832 | solution.py:73
  487.7 6.6 %fusion = bf16[32,1024]{1,0:T(8,128)(2,1)} fusion(bf16[32,4096]{1,0:T(8,128)(2,1)S(1)} %get-tuple-element.181, bf16[1024,4096]{1,0:T(8,128)(2,1)} %get-tuple-element.182, bf16[32,1024]{1,0:T(8,128)(2,1)S(1)} %get-tuple-element.180), kind=kOutput, calls=%fused_computation.1 | convolution fusion | flops 268533760 | bytes 8781824 | tf_op jit(solution)/shard_map/while/body/eval_jaxpr/cond/branch_1_fun/dot_general | solution.py:65
  494.6 10.8 %all-reduce = (bf16[4,32,64]{2,1,0:T(8,128)(2,1)S(1)}, bf16[128,64]{0,1:T(8,128)(2,1)S(1)}) all-reduce(bf16[4,32,64]{2,1,0:T(8,128)(2,1)S(1)} %bitcast.104, bf16[128,64]{0,1:T(8,128)(2,1)S(1)} %convolution_convert_fusion.1), channel_id=1, replica_groups=mesh['section'=16,'dp'=8,'mp'=4] {'mp'}, use_global_device_ids=true, to_apply=%region_5.6 | all-reduce | flops 16384 | bytes 65536 | tf_op jit(solution)/shard_map/psum | solution.py:92
  505.7 18.5 %all-gather.1 = f32[8,4,1024]{2,1,0:T(4,128)S(1)} all-gather(f32[1,4,1024]{2,1,0:T(4,128)S(1)} %broadcast_in_dim_reshape.3), channel_id=1, replica_groups=mesh['section'=16,'dp'=8,'mp'=4] {'dp'}, dimensions={0}, use_global_device_ids=true | all-gather | bytes 147456 | tf_op jit(solution)/shard_map/all_gather | solution.py:108
  529.0 99.2 %psum.23 = f32[16,8,4]{1,0,2:T(8,128)S(1)} all-reduce(f32[16,8,4]{1,0,2:T(8,128)S(1)} %bitcast.105), channel_id=1, replica_groups=mesh['section'=16,'dp'=8,'mp'=4] {'section','dp','mp'}, use_global_device_ids=true, to_apply=%region_6.7 | all-reduce | flops 512 | bytes 4096 | tf_op jit(solution)/shard_map/psum | solution.py:115
  (102 shorter events, 54.5 us)
Async XLA Ops:
  7.2 17.0 %copy-start = (bf16[1,128,1024]{2,1,0:T(8,128)(2,1)S(1)}, bf16[1,128,1024]{2,1,0:T(8,128)(2,1)}, u32[]{:S(2)}) copy-start(bf16[1,128,1024]{2,1,0:T(8,128)(2,1)} %param.13) | copy-start | bytes 786436
  7.2 106.0 %all-gather.4.cloned.1.call-start = ((), (), s32[]{:S(2)}) async-start(), calls=%async_computation | async-start | bytes 9437184 | tf_op jit(solution)/shard_map/all_gather | solution.py:46
  113.8 380.5 %copy-start.2 = (bf16[1,1024,64]{1,2,0:T(8,128)(2,1)S(1)}, bf16[1,1024,64]{1,2,0:T(8,128)(2,1)}, u32[]{:S(2)}) copy-start(bf16[1,1024,64]{1,2,0:T(8,128)(2,1)} %param.17) | copy-start | bytes 393220
  113.8 410.4 %copy-start.1 = (f32[1,2,1024]{2,1,0:T(2,128)S(1)}, f32[1,2,1024]{2,1,0:T(2,128)}, u32[]{:S(2)}) copy-start(f32[1,2,1024]{2,1,0:T(2,128)} %param.18) | copy-start | bytes 24580
  113.9 5.4 collective-permute-start
  128.2 5.6 collective-permute-start
  142.1 5.6 collective-permute-start
  155.9 6.3 collective-permute-start
  170.1 7.1 %collective-permute-start = (bf16[32,1024]{1,0:T(8,128)(2,1)}, bf16[32,1024]{1,0:T(8,128)(2,1)S(1)}, u32[]{:S(2)}, u32[]{:S(2)}) collective-permute-start(bf16[32,1024]{1,0:T(8,128)(2,1)} %get-tuple-element.299), channel_id=1, source_target_pairs={{32,0},{64,32},{96,64},{128,96},{160,128},{192,160},{224,192},{256... | collective-permute-start | bytes 196616 | tf_op jit(solution)/shard_map/while/body/eval_jaxpr/ppermute | solution.py:13
  185.2 7.1 %collective-permute-start = (bf16[32,1024]{1,0:T(8,128)(2,1)}, bf16[32,1024]{1,0:T(8,128)(2,1)S(1)}, u32[]{:S(2)}, u32[]{:S(2)}) collective-permute-start(bf16[32,1024]{1,0:T(8,128)(2,1)} %get-tuple-element.299), channel_id=1, source_target_pairs={{32,0},{64,32},{96,64},{128,96},{160,128},{192,160},{224,192},{256... | collective-permute-start | bytes 196616 | tf_op jit(solution)/shard_map/while/body/eval_jaxpr/ppermute | solution.py:13
  200.2 7.1 %collective-permute-start = (bf16[32,1024]{1,0:T(8,128)(2,1)}, bf16[32,1024]{1,0:T(8,128)(2,1)S(1)}, u32[]{:S(2)}, u32[]{:S(2)}) collective-permute-start(bf16[32,1024]{1,0:T(8,128)(2,1)} %get-tuple-element.299), channel_id=1, source_target_pairs={{32,0},{64,32},{96,64},{128,96},{160,128},{192,160},{224,192},{256... | collective-permute-start | bytes 196616 | tf_op jit(solution)/shard_map/while/body/eval_jaxpr/ppermute | solution.py:13
  215.2 7.1 %collective-permute-start = (bf16[32,1024]{1,0:T(8,128)(2,1)}, bf16[32,1024]{1,0:T(8,128)(2,1)S(1)}, u32[]{:S(2)}, u32[]{:S(2)}) collective-permute-start(bf16[32,1024]{1,0:T(8,128)(2,1)} %get-tuple-element.299), channel_id=1, source_target_pairs={{32,0},{64,32},{96,64},{128,96},{160,128},{192,160},{224,192},{256... | collective-permute-start | bytes 196616 | tf_op jit(solution)/shard_map/while/body/eval_jaxpr/ppermute | solution.py:13
  230.2 7.1 %collective-permute-start = (bf16[32,1024]{1,0:T(8,128)(2,1)}, bf16[32,1024]{1,0:T(8,128)(2,1)S(1)}, u32[]{:S(2)}, u32[]{:S(2)}) collective-permute-start(bf16[32,1024]{1,0:T(8,128)(2,1)} %get-tuple-element.299), channel_id=1, source_target_pairs={{32,0},{64,32},{96,64},{128,96},{160,128},{192,160},{224,192},{256... | collective-permute-start | bytes 196616 | tf_op jit(solution)/shard_map/while/body/eval_jaxpr/ppermute | solution.py:13
  245.3 7.1 %collective-permute-start = (bf16[32,1024]{1,0:T(8,128)(2,1)}, bf16[32,1024]{1,0:T(8,128)(2,1)S(1)}, u32[]{:S(2)}, u32[]{:S(2)}) collective-permute-start(bf16[32,1024]{1,0:T(8,128)(2,1)} %get-tuple-element.299), channel_id=1, source_target_pairs={{32,0},{64,32},{96,64},{128,96},{160,128},{192,160},{224,192},{256... | collective-permute-start | bytes 196616 | tf_op jit(solution)/shard_map/while/body/eval_jaxpr/ppermute | solution.py:13
  260.3 9.4 %collective-permute-start = (bf16[32,1024]{1,0:T(8,128)(2,1)}, bf16[32,1024]{1,0:T(8,128)(2,1)S(1)}, u32[]{:S(2)}, u32[]{:S(2)}) collective-permute-start(bf16[32,1024]{1,0:T(8,128)(2,1)} %get-tuple-element.299), channel_id=1, source_target_pairs={{32,0},{64,32},{96,64},{128,96},{160,128},{192,160},{224,192},{256... | collective-permute-start | bytes 196616 | tf_op jit(solution)/shard_map/while/body/eval_jaxpr/ppermute | solution.py:13
  277.6 9.5 %collective-permute-start = (bf16[32,1024]{1,0:T(8,128)(2,1)}, bf16[32,1024]{1,0:T(8,128)(2,1)S(1)}, u32[]{:S(2)}, u32[]{:S(2)}) collective-permute-start(bf16[32,1024]{1,0:T(8,128)(2,1)} %get-tuple-element.299), channel_id=1, source_target_pairs={{32,0},{64,32},{96,64},{128,96},{160,128},{192,160},{224,192},{256... | collective-permute-start | bytes 196616 | tf_op jit(solution)/shard_map/while/body/eval_jaxpr/ppermute | solution.py:13
  295.0 9.5 %collective-permute-start = (bf16[32,1024]{1,0:T(8,128)(2,1)}, bf16[32,1024]{1,0:T(8,128)(2,1)S(1)}, u32[]{:S(2)}, u32[]{:S(2)}) collective-permute-start(bf16[32,1024]{1,0:T(8,128)(2,1)} %get-tuple-element.299), channel_id=1, source_target_pairs={{32,0},{64,32},{96,64},{128,96},{160,128},{192,160},{224,192},{256... | collective-permute-start | bytes 196616 | tf_op jit(solution)/shard_map/while/body/eval_jaxpr/ppermute | solution.py:13
  312.4 9.5 %collective-permute-start = (bf16[32,1024]{1,0:T(8,128)(2,1)}, bf16[32,1024]{1,0:T(8,128)(2,1)S(1)}, u32[]{:S(2)}, u32[]{:S(2)}) collective-permute-start(bf16[32,1024]{1,0:T(8,128)(2,1)} %get-tuple-element.299), channel_id=1, source_target_pairs={{32,0},{64,32},{96,64},{128,96},{160,128},{192,160},{224,192},{256... | collective-permute-start | bytes 196616 | tf_op jit(solution)/shard_map/while/body/eval_jaxpr/ppermute | solution.py:13
  329.9 9.5 %collective-permute-start = (bf16[32,1024]{1,0:T(8,128)(2,1)}, bf16[32,1024]{1,0:T(8,128)(2,1)S(1)}, u32[]{:S(2)}, u32[]{:S(2)}) collective-permute-start(bf16[32,1024]{1,0:T(8,128)(2,1)} %get-tuple-element.299), channel_id=1, source_target_pairs={{32,0},{64,32},{96,64},{128,96},{160,128},{192,160},{224,192},{256... | collective-permute-start | bytes 196616 | tf_op jit(solution)/shard_map/while/body/eval_jaxpr/ppermute | solution.py:13
  347.3 62.9 %collective-permute-start = (bf16[32,1024]{1,0:T(8,128)(2,1)}, bf16[32,1024]{1,0:T(8,128)(2,1)S(1)}, u32[]{:S(2)}, u32[]{:S(2)}) collective-permute-start(bf16[32,1024]{1,0:T(8,128)(2,1)} %get-tuple-element.299), channel_id=1, source_target_pairs={{32,0},{64,32},{96,64},{128,96},{160,128},{192,160},{224,192},{256... | collective-permute-start | bytes 196616 | tf_op jit(solution)/shard_map/while/body/eval_jaxpr/ppermute | solution.py:13
  424.0 9.6 %collective-permute-start = (bf16[32,1024]{1,0:T(8,128)(2,1)}, bf16[32,1024]{1,0:T(8,128)(2,1)S(1)}, u32[]{:S(2)}, u32[]{:S(2)}) collective-permute-start(bf16[32,1024]{1,0:T(8,128)(2,1)} %get-tuple-element.299), channel_id=1, source_target_pairs={{32,0},{64,32},{96,64},{128,96},{160,128},{192,160},{224,192},{256... | collective-permute-start | bytes 196616 | tf_op jit(solution)/shard_map/while/body/eval_jaxpr/ppermute | solution.py:13
  447.4 9.6 %collective-permute-start = (bf16[32,1024]{1,0:T(8,128)(2,1)}, bf16[32,1024]{1,0:T(8,128)(2,1)S(1)}, u32[]{:S(2)}, u32[]{:S(2)}) collective-permute-start(bf16[32,1024]{1,0:T(8,128)(2,1)} %get-tuple-element.299), channel_id=1, source_target_pairs={{32,0},{64,32},{96,64},{128,96},{160,128},{192,160},{224,192},{256... | collective-permute-start | bytes 196616 | tf_op jit(solution)/shard_map/while/body/eval_jaxpr/ppermute | solution.py:13
  470.9 9.6 %collective-permute-start = (bf16[32,1024]{1,0:T(8,128)(2,1)}, bf16[32,1024]{1,0:T(8,128)(2,1)S(1)}, u32[]{:S(2)}, u32[]{:S(2)}) collective-permute-start(bf16[32,1024]{1,0:T(8,128)(2,1)} %get-tuple-element.299), channel_id=1, source_target_pairs={{32,0},{64,32},{96,64},{128,96},{160,128},{192,160},{224,192},{256... | collective-permute-start | bytes 196616 | tf_op jit(solution)/shard_map/while/body/eval_jaxpr/ppermute | solution.py:13
  505.7 123.2 %copy-start.3 = (f32[1,4,1024]{2,1,0:T(4,128)}, f32[1,4,1024]{2,1,0:T(4,128)S(1)}, u32[]{:S(2)}) copy-start(f32[1,4,1024]{2,1,0:T(4,128)S(1)} %broadcast_in_dim_reshape.3) | copy-start | bytes 49156
Sparse Core Ops, SparseCore 0:
  10.1 103.0 all-gather.3
where the time goes:
time: 638 us; the launch traced here: 636 us
  waiting for transfers between devices  268 us (42%)
  blocking collectives  251 us (39%)
  matrix products  29.3 us (5%)
  between operations  28.8 us (5%)
  starting transfers between devices  24.5 us (4%)
  other arithmetic  18.2 us (3%)
  local copies, waits for them, and re-layouts  15.9 us (2%)
    ppermute x19, waiting for transfers between devices, from_behind(): return lax.ppermute(block, axis, route)  179 us
    all_gather x19, blocking collectives, advance(): grad_full = lax.all_gather(grad_piece, 'mp', axis=1, tiled=True)  122 us
    psum x1, blocking collectives, body(): summed = lax.psum(score_table * score_scale, ('section', 'dp', 'mp'))  99.2 us
    all_gather x1, waiting for transfers between devices, body(): w_rows = lax.all_gather(weights[0], 'dp', axis=1, tiled=True)  87.9 us
    dot_general x4, matrix products, through(): lax.dot_general(grad_full, w_rows, (((1,), (1,)), ((), ())), preferred_el...  26.4 us
    ppermute x19, starting transfers between devices, from_behind(): return lax.ppermute(block, axis, route)  24.5 us
    all_gather x1, blocking collectives, body(): lax.all_gather(panels_here, 'dp', axis=0, tiled=True)  18.5 us
    dynamic_update_slice x19, other arithmetic, advance(): lax.dynamic_update_slice_in_dim(stored, jnp.where(active, grad_piece, pre...  18.2 us
  transfers between devices with their start and end apart: 20, of which 20 were waited for; matrix products, arithmetic and copies ran while one was open for 0% of the time, Pallas kernels for 0%

commit v1 on v0

--- a/solution.py
+++ b/solution.py
@@ -5,6 +5,16 @@
 from jax.sharding import PartitionSpec as P
 
 LEN = 32
+
+
+def gather_by_hops(x, mesh_axis, dim):
+    size = lax.axis_size(mesh_axis)
+    held, shards = (x, [x])
+    for _ in range(size - 1):
+        held = lax.ppermute(held, mesh_axis, [(i, (i + 1) % size) for i in range(size)])
+        shards.insert(0, held)
+    flat = jnp.concatenate(shards, axis=dim)
+    return jnp.roll(flat, (lax.axis_index(mesh_axis) + 1) * x.shape[dim], axis=dim)
 
 
 def from_behind(block, axis, distance):
@@ -43,7 +53,7 @@
     length = LEN
     examples = inputs.shape[0] // length
     low_rank = proj_in.shape[2]
-    w_rows = lax.all_gather(weights[0], "dp", axis=1, tiled=True)
+    w_rows = gather_by_hops(weights[0], "dp", 1)
     step_count = examples + section_count - 1
     top_section = section_count - 1
 

time: 638 us -> 743 us (1.16)
  waiting for transfers between devices: 268 us -> 325 us
  local copies, waits for them, and re-layouts: 15.9 us -> 53.7 us
  starting transfers between devices: 24.5 us -> 40.9 us
  between operations: 28.8 us -> 15.9 us
    ppermute x0 -> x7, waiting for transfers between devices: none -> 146 us  [gather_by_hops(): lax.ppermute(held, mesh_axis, [(i, (i + 1) % size) for i in range(size)])]
    all_gather x1 -> x0, waiting for transfers between devices: 87.9 us -> none  [body(): w_rows = lax.all_gather(weights[0], 'dp', axis=1, tiled=True)]
    unnamed x9 -> x38, local copies, waits for them, and re-layouts: 0.7 us -> 29.6 us
    ppermute x0 -> x7, starting transfers between devices: none -> 16.4 us  [gather_by_hops(): lax.ppermute(held, mesh_axis, [(i, (i + 1) % size) for i in range(size)])]
    dynamic_slice x0 -> x1, local copies, waits for them, and re-layouts: none -> 7.73 us  [gather_by_hops(): jnp.roll(flat, (lax.axis_index(mesh_axis) + 1) * x.shape[dim], axis=dim)]
  transfers between devices with their start and end apart: 20 -> 26, of which waited for: 20 -> 26; matrix products, arithmetic and copies ran while one was open for 0% -> 0% of each run, Pallas kernels for 0% -> 0%
where the time goes in v1:
time: 743 us; the launch traced here: 740 us
  waiting for transfers between devices  325 us (44%)
  blocking collectives  256 us (34%)
  local copies, waits for them, and re-layouts  53.7 us (7%)
  starting transfers between devices  40.9 us (6%)
  matrix products  29.5 us (4%)
  other arithmetic  18.2 us (2%)
  between operations  15.9 us (2%)
    ppermute x19, waiting for transfers between devices, from_behind(): return lax.ppermute(block, axis, route)  180 us
    ppermute x7, waiting for transfers between devices, gather_by_hops(): lax.ppermute(held, mesh_axis, [(i, (i + 1) % size) for i in range(size)])  146 us
    all_gather x19, blocking collectives, advance(): grad_full = lax.all_gather(grad_piece, 'mp', axis=1, tiled=True)  129 us
    psum x1, blocking collectives, body(): summed = lax.psum(score_table * score_scale, ('section', 'dp', 'mp'))  98.5 us
    unnamed x38, local copies, waits for them, and re-layouts  29.6 us
    dot_general x4, matrix products, through(): lax.dot_general(grad_full, w_rows, (((1,), (1,)), ((), ())), preferred_el...  26.4 us
    ppermute x19, starting transfers between devices, from_behind(): return lax.ppermute(block, axis, route)  24.5 us
    all_gather x1, blocking collectives, body(): lax.all_gather(panels_here, 'dp', axis=0, tiled=True)  18.3 us
  transfers between devices with their start and end apart: 26, of which 26 were waited for; matrix products, arithmetic and copies ran while one was open for 0% of the time, Pallas kernels for 0%

profile of v1, /device:TPU:1, one launch (start us, length us, event | category | flops | bytes accessed | tf_op | source)
XLA Modules:
  0.0 740.5 jit_solution(1612153399826048279)
XLA Ops:
  0.7 5.0 collective-permute-start.1
  5.6 29.7 %collective-permute-done.1 = bf16[1024,512]{1,0:T(8,128)(2,1)S(1)} collective-permute-done((bf16[1024,512]{1,0:T(8,128)(2,1)}, bf16[1024,512]{1,0:T(8,128)(2,1)S(1)}, u32[]{:S(2)}, u32[]{:S(2)}) %collective-permute-start.1) | collective-permute-done | bytes 1048608 | tf_op jit(solution)/shard_map/ppermute | solution.py:14
  37.3 24.6 %collective-permute-done.2 = bf16[1024,512]{1,0:T(8,128)(2,1)S(1)} collective-permute-done((bf16[1024,512]{1,0:T(8,128)(2,1)S(1)}, bf16[1024,512]{1,0:T(8,128)(2,1)S(1)}, u32[]{:S(2)}, u32[]{:S(2)}) %collective-permute-start.2) | collective-permute-done | bytes 1048608 | tf_op jit(solution)/shard_map/ppermute | solution.py:14
  63.8 23.7 %collective-permute-done.3 = bf16[1024,512]{1,0:T(8,128)(2,1)S(1)} collective-permute-done((bf16[1024,512]{1,0:T(8,128)(2,1)S(1)}, bf16[1024,512]{1,0:T(8,128)(2,1)S(1)}, u32[]{:S(2)}, u32[]{:S(2)}) %collective-permute-start.3) | collective-permute-done | bytes 1048608 | tf_op jit(solution)/shard_map/ppermute | solution.py:14
  90.4 22.8 %collective-permute-done.4 = bf16[1024,512]{1,0:T(8,128)(2,1)S(1)} collective-permute-done((bf16[1024,512]{1,0:T(8,128)(2,1)S(1)}, bf16[1024,512]{1,0:T(8,128)(2,1)S(1)}, u32[]{:S(2)}, u32[]{:S(2)}) %collective-permute-start.4) | collective-permute-done | bytes 1048608 | tf_op jit(solution)/shard_map/ppermute | solution.py:14
  116.0 21.8 %collective-permute-done.5 = bf16[1024,512]{1,0:T(8,128)(2,1)S(1)} collective-permute-done((bf16[1024,512]{1,0:T(8,128)(2,1)S(1)}, bf16[1024,512]{1,0:T(8,128)(2,1)S(1)}, u32[]{:S(2)}, u32[]{:S(2)}) %collective-permute-start.5) | collective-permute-done | bytes 1048608 | tf_op jit(solution)/shard_map/ppermute | solution.py:14
  140.8 21.0 %collective-permute-done.6 = bf16[1024,512]{1,0:T(8,128)(2,1)} collective-permute-done((bf16[1024,512]{1,0:T(8,128)(2,1)S(1)}, bf16[1024,512]{1,0:T(8,128)(2,1)}, u32[]{:S(2)}, u32[]{:S(2)}) %collective-permute-start.6) | collective-permute-done | bytes 1048608 | tf_op jit(solution)/shard_map/ppermute | solution.py:14
  186.3 2.3 constant_dynamic-update-slice_fusion.14
  188.6 2.3 constant_dynamic-update-slice_fusion.13
  193.1 2.3 constant_dynamic-update-slice_fusion.11
  197.5 2.3 constant_dynamic-update-slice_fusion.8
  199.8 2.3 constant_dynamic-update-slice_fusion.7
  202.2 2.3 constant_dynamic-update-slice_fusion.6
  211.1 7.7 %constant_dynamic-slice_fusion.1 = bf16[1024,4096]{1,0:T(8,128)(2,1)} fusion(bf16[1024,8192]{1,0:T(8,128)(2,1)} %constant_dynamic-update-slice_fusion, s32[]{:T(128)S(6)} %select_n.111), kind=kLoop, calls=%fused_computation.78 | loop fusion | bytes 16777220 | tf_op jit(solution)/shard_map/jit(_roll_dynamic)/dynamic_slice | solution.py:17
  219.4 387.3 %while.17 = (s32[]{:T(128)}, bf16[32,1024]{1,0:T(8,128)(2,1)}, bf16[128,1024]{1,0:T(8,128)(2,1)S(1)}, s32[]{:T(128)}, pred[]{:T(512)}, /*index=5*/bf16[128,1024]...) while((s32[]{:T(128)}, bf16[32,1024]{1,0:T(8,128)(2,1)}, ...), condition=%wide.region_4.5_spmd, body=%wide.region_1.4_spmd.sunk | while | flops 268959744 | bytes 9830719 | solution.py:95
  220.9 3.9 collective-permute-done
  225.7 13.5 %all_gather.14 = bf16[32,4096]{1,0:T(8,128)(2,1)S(1)} all-gather(bf16[32,1024]{1,0:T(8,128)(2,1)S(1)} %get-tuple-element.282), channel_id=1, replica_groups=mesh['section'=16,'dp'=8,'mp'=4] {'mp'}, dimensions={1}, use_global_device_ids=true | all-gather | bytes 327680 | tf_op jit(solution)/shard_map/while/body/eval_jaxpr/all_gather | solution.py:72
  241.2 4.3 collective-permute-done
  246.5 6.6 all_gather.14
  255.0 4.3 collective-permute-done
  260.3 6.6 all_gather.14
  268.9 5.3 collective-permute-done
  275.1 6.4 all_gather.14
  283.4 5.8 collective-permute-done
  290.1 6.4 all_gather.14
  298.4 5.8 collective-permute-done
  305.2 6.4 all_gather.14
  313.5 5.8 collective-permute-done
  320.2 6.4 all_gather.14
  328.5 5.8 collective-permute-done
  335.2 6.4 all_gather.14
  343.5 5.8 collective-permute-done
  350.3 6.4 all_gather.14
  358.6 6.0 collective-permute-done
  365.5 6.4 all_gather.14
  373.8 8.2 %collective-permute-done = bf16[32,1024]{1,0:T(8,128)(2,1)S(1)} collective-permute-done((bf16[32,1024]{1,0:T(8,128)(2,1)}, bf16[32,1024]{1,0:T(8,128)(2,1)S(1)}, u32[]{:S(2)}, u32[]{:S(2)}) %collective-permute-start) | collective-permute-done | bytes 65568 | tf_op jit(solution)/shard_map/while/body/eval_jaxpr/ppermute | solution.py:23
  383.0 6.4 all_gather.14
  391.3 8.2 %collective-permute-done = bf16[32,1024]{1,0:T(8,128)(2,1)S(1)} collective-permute-done((bf16[32,1024]{1,0:T(8,128)(2,1)}, bf16[32,1024]{1,0:T(8,128)(2,1)S(1)}, u32[]{:S(2)}, u32[]{:S(2)}) %collective-permute-start) | collective-permute-done | bytes 65568 | tf_op jit(solution)/shard_map/while/body/eval_jaxpr/ppermute | solution.py:23
  400.4 6.4 all_gather.14
  408.7 8.2 %collective-permute-done = bf16[32,1024]{1,0:T(8,128)(2,1)S(1)} collective-permute-done((bf16[32,1024]{1,0:T(8,128)(2,1)}, bf16[32,1024]{1,0:T(8,128)(2,1)S(1)}, u32[]{:S(2)}, u32[]{:S(2)}) %collective-permute-start) | collective-permute-done | bytes 65568 | tf_op jit(solution)/shard_map/while/body/eval_jaxpr/ppermute | solution.py:23
  417.8 6.4 all_gather.14
  426.1 8.2 %collective-permute-done = bf16[32,1024]{1,0:T(8,128)(2,1)S(1)} collective-permute-done((bf16[32,1024]{1,0:T(8,128)(2,1)}, bf16[32,1024]{1,0:T(8,128)(2,1)S(1)}, u32[]{:S(2)}, u32[]{:S(2)}) %collective-permute-start) | collective-permute-done | bytes 65568 | tf_op jit(solution)/shard_map/while/body/eval_jaxpr/ppermute | solution.py:23
  435.3 6.4 all_gather.14
  443.6 8.2 %collective-permute-done = bf16[32,1024]{1,0:T(8,128)(2,1)S(1)} collective-permute-done((bf16[32,1024]{1,0:T(8,128)(2,1)}, bf16[32,1024]{1,0:T(8,128)(2,1)S(1)}, u32[]{:S(2)}, u32[]{:S(2)}) %collective-permute-start) | collective-permute-done | bytes 65568 | tf_op jit(solution)/shard_map/while/body/eval_jaxpr/ppermute | solution.py:23
  452.7 6.4 all_gather.14
  461.0 61.5 %collective-permute-done = bf16[32,1024]{1,0:T(8,128)(2,1)S(1)} collective-permute-done((bf16[32,1024]{1,0:T(8,128)(2,1)}, bf16[32,1024]{1,0:T(8,128)(2,1)S(1)}, u32[]{:S(2)}, u32[]{:S(2)}) %collective-permute-start) | collective-permute-done | bytes 65568 | tf_op jit(solution)/shard_map/while/body/eval_jaxpr/ppermute | solution.py:23
  523.5 6.4 all_gather.14
  529.9 6.6 conditional.2
  529.9 6.6 fusion
  537.8 8.2 %collective-permute-done = bf16[32,1024]{1,0:T(8,128)(2,1)S(1)} collective-permute-done((bf16[32,1024]{1,0:T(8,128)(2,1)}, bf16[32,1024]{1,0:T(8,128)(2,1)S(1)}, u32[]{:S(2)}, u32[]{:S(2)}) %collective-permute-start) | collective-permute-done | bytes 65568 | tf_op jit(solution)/shard_map/while/body/eval_jaxpr/ppermute | solution.py:23
  546.9 6.4 all_gather.14
  553.3 6.6 conditional.2
  553.3 6.6 fusion
  561.2 8.2 %collective-permute-done = bf16[32,1024]{1,0:T(8,128)(2,1)S(1)} collective-permute-done((bf16[32,1024]{1,0:T(8,128)(2,1)}, bf16[32,1024]{1,0:T(8,128)(2,1)S(1)}, u32[]{:S(2)}, u32[]{:S(2)}) %collective-permute-start) | collective-permute-done | bytes 65568 | tf_op jit(solution)/shard_map/while/body/eval_jaxpr/ppermute | solution.py:23
  570.3 6.4 all_gather.14
  576.7 6.6 conditional.2
  576.7 6.6 fusion
  584.6 8.2 %collective-permute-done = bf16[32,1024]{1,0:T(8,128)(2,1)S(1)} collective-permute-done((bf16[32,1024]{1,0:T(8,128)(2,1)}, bf16[32,1024]{1,0:T(8,128)(2,1)S(1)}, u32[]{:S(2)}, u32[]{:S(2)}) %collective-permute-start) | collective-permute-done | bytes 65568 | tf_op jit(solution)/shard_map/while/body/eval_jaxpr/ppermute | solution.py:23
  593.7 6.4 all_gather.14
  600.1 6.6 conditional.2
  600.1 6.6 fusion
  607.1 10.8 %all-reduce = (bf16[4,32,64]{2,1,0:T(8,128)(2,1)S(1)}, bf16[128,64]{0,1:T(8,128)(2,1)S(1)}) all-reduce(bf16[4,32,64]{2,1,0:T(8,128)(2,1)S(1)} %bitcast.106, bf16[128,64]{0,1:T(8,128)(2,1)S(1)} %convolution_convert_fusion.1), channel_id=1, replica_groups=mesh['section'=16,'dp'=8,'mp'=4] {'mp'}, use_global_device_ids=true, to_apply=%region_5.6 | all-reduce | flops 16384 | bytes 65536 | tf_op jit(solution)/shard_map/psum | solution.py:102
  618.2 18.3 %all-gather = f32[8,4,1024]{2,1,0:T(4,128)S(1)} all-gather(f32[1,4,1024]{2,1,0:T(4,128)S(1)} %broadcast_in_dim_reshape.3), channel_id=1, replica_groups=mesh['section'=16,'dp'=8,'mp'=4] {'dp'}, dimensions={0}, use_global_device_ids=true | all-gather | bytes 147456 | tf_op jit(solution)/shard_map/all_gather | solution.py:118
  641.2 98.5 %psum.23 = f32[16,8,4]{1,0,2:T(8,128)S(1)} all-reduce(f32[16,8,4]{1,0,2:T(8,128)S(1)} %bitcast.107), channel_id=1, replica_groups=mesh['section'=16,'dp'=8,'mp'=4] {'section','dp','mp'}, use_global_device_ids=true, to_apply=%region_6.7 | all-reduce | flops 512 | bytes 4096 | tf_op jit(solution)/shard_map/psum | solution.py:125
  (144 shorter events, 101.2 us)
Async XLA Ops:
  0.6 179.8 %copy-start = (bf16[1,128,1024]{2,1,0:T(8,128)(2,1)S(1)}, bf16[1,128,1024]{2,1,0:T(8,128)(2,1)}, u32[]{:S(2)}) copy-start(bf16[1,128,1024]{2,1,0:T(8,128)(2,1)} %param.13) | copy-start | bytes 786436
  0.6 209.3 %copy-start.1 = (bf16[1,1024,512]{2,1,0:T(8,128)(2,1)S(1)}, bf16[1,1024,512]{2,1,0:T(8,128)(2,1)}, u32[]{:S(2)}) copy-start(bf16[1,1024,512]{2,1,0:T(8,128)(2,1)} %param.15) | copy-start | bytes 3145732
  0.7 34.7 %collective-permute-start.1 = (bf16[1024,512]{1,0:T(8,128)(2,1)}, bf16[1024,512]{1,0:T(8,128)(2,1)S(1)}, u32[]{:S(2)}, u32[]{:S(2)}) collective-permute-start(bf16[1024,512]{1,0:T(8,128)(2,1)} %bitcast.104), channel_id=1, source_target_pairs={{0,4},{4,8},{8,12},{12,16},{16,20},{20,24},{24,28},{28,0},{1,5},{5... | collective-permute-start | bytes 3145736 | tf_op jit(solution)/shard_map/ppermute | solution.py:14
  35.4 26.5 %collective-permute-start.2 = (bf16[1024,512]{1,0:T(8,128)(2,1)S(1)}, bf16[1024,512]{1,0:T(8,128)(2,1)S(1)}, u32[]{:S(2)}, u32[]{:S(2)}) collective-permute-start(bf16[1024,512]{1,0:T(8,128)(2,1)S(1)} %collective-permute-done.1), channel_id=1, source_target_pairs={{0,4},{4,8},{8,12},{12,16},{16,20},{20,24},{24,28},{28,0},{1,5},{5... | collective-permute-start | bytes 3145736 | tf_op jit(solution)/shard_map/ppermute | solution.py:14
  61.9 25.6 %collective-permute-start.3 = (bf16[1024,512]{1,0:T(8,128)(2,1)S(1)}, bf16[1024,512]{1,0:T(8,128)(2,1)S(1)}, u32[]{:S(2)}, u32[]{:S(2)}) collective-permute-start(bf16[1024,512]{1,0:T(8,128)(2,1)S(1)} %collective-permute-done.2), channel_id=1, source_target_pairs={{0,4},{4,8},{8,12},{12,16},{16,20},{20,24},{24,28},{28,0},{1,5},{5... | collective-permute-start | bytes 3145736 | tf_op jit(solution)/shard_map/ppermute | solution.py:14
  87.5 1.0 copy-start.2
  88.5 24.7 %collective-permute-start.4 = (bf16[1024,512]{1,0:T(8,128)(2,1)S(1)}, bf16[1024,512]{1,0:T(8,128)(2,1)S(1)}, u32[]{:S(2)}, u32[]{:S(2)}) collective-permute-start(bf16[1024,512]{1,0:T(8,128)(2,1)S(1)} %collective-permute-done.3), channel_id=1, source_target_pairs={{0,4},{4,8},{8,12},{12,16},{16,20},{20,24},{24,28},{28,0},{1,5},{5... | collective-permute-start | bytes 3145736 | tf_op jit(solution)/shard_map/ppermute | solution.py:14
  113.1 1.0 copy-start.4
  114.1 23.8 %collective-permute-start.5 = (bf16[1024,512]{1,0:T(8,128)(2,1)S(1)}, bf16[1024,512]{1,0:T(8,128)(2,1)S(1)}, u32[]{:S(2)}, u32[]{:S(2)}) collective-permute-start(bf16[1024,512]{1,0:T(8,128)(2,1)S(1)} %collective-permute-done.4), channel_id=1, source_target_pairs={{0,4},{4,8},{8,12},{12,16},{16,20},{20,24},{24,28},{28,0},{1,5},{5... | collective-permute-start | bytes 3145736 | tf_op jit(solution)/shard_map/ppermute | solution.py:14
  137.9 1.0 copy-start.6
  138.8 22.9 %collective-permute-start.6 = (bf16[1024,512]{1,0:T(8,128)(2,1)S(1)}, bf16[1024,512]{1,0:T(8,128)(2,1)}, u32[]{:S(2)}, u32[]{:S(2)}) collective-permute-start(bf16[1024,512]{1,0:T(8,128)(2,1)S(1)} %collective-permute-done.5), channel_id=1, source_target_pairs={{0,4},{4,8},{8,12},{12,16},{16,20},{20,24},{24,28},{28,0},{1,5},{5... | collective-permute-start | bytes 3145736 | tf_op jit(solution)/shard_map/ppermute | solution.py:14
  161.8 22.2 %collective-permute-start.7 = (bf16[1024,512]{1,0:T(8,128)(2,1)}, bf16[1024,512]{1,0:T(8,128)(2,1)}, u32[]{:S(2)}, u32[]{:S(2)}) collective-permute-start(bf16[1024,512]{1,0:T(8,128)(2,1)} %collective-permute-done.6), channel_id=1, source_target_pairs={{0,4},{4,8},{8,12},{12,16},{16,20},{20,24},{24,28},{28,0},{1,5},{5... | collective-permute-start | bytes 3145736 | tf_op jit(solution)/shard_map/ppermute | solution.py:14
  180.5 24.0 %copy-start.7 = (bf16[1024,512]{1,0:T(8,128)(2,1)S(1)}, bf16[1024,512]{1,0:T(8,128)(2,1)}, u32[]{:S(2)}) copy-start(bf16[1024,512]{1,0:T(8,128)(2,1)} %copy-done.6) | copy-start | bytes 3145732
  180.5 25.1 %copy-start.5 = (bf16[1024,512]{1,0:T(8,128)(2,1)S(1)}, bf16[1024,512]{1,0:T(8,128)(2,1)}, u32[]{:S(2)}) copy-start(bf16[1024,512]{1,0:T(8,128)(2,1)} %copy-done.4) | copy-start | bytes 3145732
  180.5 26.2 %copy-start.3 = (bf16[1024,512]{1,0:T(8,128)(2,1)S(1)}, bf16[1024,512]{1,0:T(8,128)(2,1)}, u32[]{:S(2)}) copy-start(bf16[1024,512]{1,0:T(8,128)(2,1)} %copy-done.2) | copy-start | bytes 3145732
  219.4 387.3 %copy-start.9 = (bf16[1,1024,64]{1,2,0:T(8,128)(2,1)S(1)}, bf16[1,1024,64]{1,2,0:T(8,128)(2,1)}, u32[]{:S(2)}) copy-start(bf16[1,1024,64]{1,2,0:T(8,128)(2,1)} %param.17) | copy-start | bytes 393220
  219.4 417.0 %copy-start.8 = (f32[1,2,1024]{2,1,0:T(2,128)S(1)}, f32[1,2,1024]{2,1,0:T(2,128)}, u32[]{:S(2)}) copy-start(f32[1,2,1024]{2,1,0:T(2,128)} %param.18) | copy-start | bytes 24580
  219.4 5.3 collective-permute-start
  239.9 5.6 collective-permute-start
  253.7 5.6 collective-permute-start
  267.6 6.6 collective-permute-start
  282.1 7.1 collective-permute-start
  297.1 7.1 collective-permute-start
  312.2 7.1 collective-permute-start
  327.2 7.1 collective-permute-start
  342.2 7.1 collective-permute-start
  357.3 7.3 collective-permute-start
  372.5 9.5 %collective-permute-start = (bf16[32,1024]{1,0:T(8,128)(2,1)}, bf16[32,1024]{1,0:T(8,128)(2,1)S(1)}, u32[]{:S(2)}, u32[]{:S(2)}) collective-permute-start(bf16[32,1024]{1,0:T(8,128)(2,1)} %get-tuple-element.299), channel_id=1, source_target_pairs={{32,0},{64,32},{96,64},{128,96},{160,128},{192,160},{224,192},{256... | collective-permute-start | bytes 196616 | tf_op jit(solution)/shard_map/while/body/eval_jaxpr/ppermute | solution.py:23
  390.0 9.5 %collective-permute-start = (bf16[32,1024]{1,0:T(8,128)(2,1)}, bf16[32,1024]{1,0:T(8,128)(2,1)S(1)}, u32[]{:S(2)}, u32[]{:S(2)}) collective-permute-start(bf16[32,1024]{1,0:T(8,128)(2,1)} %get-tuple-element.299), channel_id=1, source_target_pairs={{32,0},{64,32},{96,64},{128,96},{160,128},{192,160},{224,192},{256... | collective-permute-start | bytes 196616 | tf_op jit(solution)/shard_map/while/body/eval_jaxpr/ppermute | solution.py:23
  407.4 9.5 %collective-permute-start = (bf16[32,1024]{1,0:T(8,128)(2,1)}, bf16[32,1024]{1,0:T(8,128)(2,1)S(1)}, u32[]{:S(2)}, u32[]{:S(2)}) collective-permute-start(bf16[32,1024]{1,0:T(8,128)(2,1)} %get-tuple-element.299), channel_id=1, source_target_pairs={{32,0},{64,32},{96,64},{128,96},{160,128},{192,160},{224,192},{256... | collective-permute-start | bytes 196616 | tf_op jit(solution)/shard_map/while/body/eval_jaxpr/ppermute | solution.py:23
  424.8 9.5 %collective-permute-start = (bf16[32,1024]{1,0:T(8,128)(2,1)}, bf16[32,1024]{1,0:T(8,128)(2,1)S(1)}, u32[]{:S(2)}, u32[]{:S(2)}) collective-permute-start(bf16[32,1024]{1,0:T(8,128)(2,1)} %get-tuple-element.299), channel_id=1, source_target_pairs={{32,0},{64,32},{96,64},{128,96},{160,128},{192,160},{224,192},{256... | collective-permute-start | bytes 196616 | tf_op jit(solution)/shard_map/while/body/eval_jaxpr/ppermute | solution.py:23
  442.3 9.5 %collective-permute-start = (bf16[32,1024]{1,0:T(8,128)(2,1)}, bf16[32,1024]{1,0:T(8,128)(2,1)S(1)}, u32[]{:S(2)}, u32[]{:S(2)}) collective-permute-start(bf16[32,1024]{1,0:T(8,128)(2,1)} %get-tuple-element.299), channel_id=1, source_target_pairs={{32,0},{64,32},{96,64},{128,96},{160,128},{192,160},{224,192},{256... | collective-permute-start | bytes 196616 | tf_op jit(solution)/shard_map/while/body/eval_jaxpr/ppermute | solution.py:23
  459.7 62.8 %collective-permute-start = (bf16[32,1024]{1,0:T(8,128)(2,1)}, bf16[32,1024]{1,0:T(8,128)(2,1)S(1)}, u32[]{:S(2)}, u32[]{:S(2)}) collective-permute-start(bf16[32,1024]{1,0:T(8,128)(2,1)} %get-tuple-element.299), channel_id=1, source_target_pairs={{32,0},{64,32},{96,64},{128,96},{160,128},{192,160},{224,192},{256... | collective-permute-start | bytes 196616 | tf_op jit(solution)/shard_map/while/body/eval_jaxpr/ppermute | solution.py:23
  536.5 9.5 %collective-permute-start = (bf16[32,1024]{1,0:T(8,128)(2,1)}, bf16[32,1024]{1,0:T(8,128)(2,1)S(1)}, u32[]{:S(2)}, u32[]{:S(2)}) collective-permute-start(bf16[32,1024]{1,0:T(8,128)(2,1)} %get-tuple-element.299), channel_id=1, source_target_pairs={{32,0},{64,32},{96,64},{128,96},{160,128},{192,160},{224,192},{256... | collective-permute-start | bytes 196616 | tf_op jit(solution)/shard_map/while/body/eval_jaxpr/ppermute | solution.py:23
  559.9 9.5 %collective-permute-start = (bf16[32,1024]{1,0:T(8,128)(2,1)}, bf16[32,1024]{1,0:T(8,128)(2,1)S(1)}, u32[]{:S(2)}, u32[]{:S(2)}) collective-permute-start(bf16[32,1024]{1,0:T(8,128)(2,1)} %get-tuple-element.299), channel_id=1, source_target_pairs={{32,0},{64,32},{96,64},{128,96},{160,128},{192,160},{224,192},{256... | collective-permute-start | bytes 196616 | tf_op jit(solution)/shard_map/while/body/eval_jaxpr/ppermute | solution.py:23
  583.3 9.5 %collective-permute-start = (bf16[32,1024]{1,0:T(8,128)(2,1)}, bf16[32,1024]{1,0:T(8,128)(2,1)S(1)}, u32[]{:S(2)}, u32[]{:S(2)}) collective-permute-start(bf16[32,1024]{1,0:T(8,128)(2,1)} %get-tuple-element.299), channel_id=1, source_target_pairs={{32,0},{64,32},{96,64},{128,96},{160,128},{192,160},{224,192},{256... | collective-permute-start | bytes 196616 | tf_op jit(solution)/shard_map/while/body/eval_jaxpr/ppermute | solution.py:23
  618.2 122.3 %copy-start.10 = (f32[1,4,1024]{2,1,0:T(4,128)}, f32[1,4,1024]{2,1,0:T(4,128)S(1)}, u32[]{:S(2)}) copy-start(f32[1,4,1024]{2,1,0:T(4,128)S(1)} %broadcast_in_dim_reshape.3) | copy-start | bytes 49156
